TPU v7x, 32 devices: a whole 2x2x4 slice. The times are simulated.
32 devices in a mesh: seq: 16 (over z, y, x), grp: 2 (over core).
Axes of the slice: x: 2, y: 2, z: 4, core: 2. Of those that a mesh axis runs over, the one named last changes fastest.
Arguments:
- queries: bfloat16 [4096, 2048], P('seq', 'grp'), parts along dimension 1, may hold values from -80 to 80
- shared_keys: bfloat16 [4096, 256], P('seq', 'grp'), parts along dimension 1, may hold values from -4 to 4
- shared_values: bfloat16 [4096, 256], P('seq', 'grp'), parts along dimension 1, may hold values from -6 to 6
- outputs: bfloat16 [4096, 2048], P('seq', 'grp'), parts along dimension 1, may hold values from -6 to 6
- out_grad: bfloat16 [4096, 2048], P('seq', 'grp'), parts along dimension 1, may hold values from -6 to 6
- doc_lengths: int32 [64], replicated, may hold values from 1 to 2048, 4096 in all
Outputs:
- grad_queries: bfloat16 [4096, 2048], P('seq', 'grp'), parts along dimension 1
- grad_keys: bfloat16 [4096, 256], P('seq', 'grp'), parts along dimension 1
- grad_values: bfloat16 [4096, 256], P('seq', 'grp'), parts along dimension 1
There are 2 independent parts, one for each index of `grp`. A program takes and returns all parts, laid end to end along the dimension named above; an argument that names none is the same for every part. Nothing has to cross between parts.
Inputs may be any that keep to these rules, and one draw needn't show every extreme that they name: `doc_lengths`: lengths of the 64 documents in packing order; they sum to 4096 and the longest is exactly 2048.
All inputs are finite; a program needn't handle non-finite values.
Results may differ from a plain program's by a relative error of at most 0.0051.
Values may be sent and summed in bfloat16 or wider, within the bound.
No kernel may reach another device: no remote copies, remote signals or barrier semaphores. Data moves between devices by JAX's collectives and lax.ppermute only.
A program may use at most 64 MiB of HBM per device.

v0:
```python
import jax
import jax.numpy as jnp
from jax import lax
from jax.sharding import PartitionSpec as P

REACH = 16


def from_behind(shard, axis, by):
    peers = lax.axis_size(axis)
    pairs = [(i, i + by) for i in range(peers) if 0 <= i + by < peers]
    return lax.ppermute(shard, axis, pairs)


def body(queries, shared_keys, shared_values, outputs, out_grad, doc_lengths):
    device_rank = lax.axis_index("seq")
    seq_count = lax.axis_size("seq")
    block_rows = shared_keys.shape[0] // 2
    head_width = shared_keys.shape[1]
    head_count = queries.shape[1] // head_width
    row_count = block_rows * head_count
    scaling = head_width ** (-0.5)
    doc_ends = jnp.cumsum(doc_lengths)
    doc_starts = doc_ends - doc_lengths
    own_blocks = jnp.stack([device_rank, 2 * seq_count - 1 - device_rank])
    keys_values = jnp.concatenate([shared_keys, shared_values], axis=1)

    def advance(state_pair, unused):
        lower_buf, upper_buf = state_pair
        got_lower = from_behind(lower_buf, "seq", 1)
        got_upper = from_behind(upper_buf, "seq", -1)
        got_upper = jnp.where(device_rank == seq_count - 1, lower_buf, got_upper)
        return ((got_lower, got_upper), (got_lower, got_upper))

    initial_pair = (keys_values[:block_rows], keys_values[block_rows:])
    unused_carry, (more_lower, more_upper) = lax.scan(advance, initial_pair, None, length=REACH)
    stacks = (
        jnp.concatenate([initial_pair[0][None], more_lower], axis=0),
        jnp.concatenate([initial_pair[1][None], more_upper], axis=0),
    )
    query_rows = queries.reshape(2, row_count, head_width)
    grad_rows = out_grad.reshape(2, row_count, head_width)
    products = (out_grad.astype(jnp.float32) * outputs.astype(jnp.float32)).reshape(
        2, row_count, head_width
    )
    deltas = jnp.sum(products, axis=2)
    base_pos = jnp.arange(block_rows, dtype=jnp.int32)
    query_pos = []
    query_begin = []
    for side_index in range(2):
        block_pos = own_blocks[side_index] * block_rows + base_pos
        query_pos.append(jnp.repeat(block_pos, head_count))
        query_begin.append(
            jnp.repeat(
                jnp.max(
                    jnp.where(doc_starts[None, :] <= block_pos[:, None], doc_starts[None, :], 0),
                    axis=1,
                ),
                head_count,
            )
        )

    def block_mask(side_index, offset):
        key_pos = (own_blocks[side_index] - offset) * block_rows + base_pos
        return (key_pos[None, :] >= query_begin[side_index][:, None]) & (
            key_pos[None, :] <= query_pos[side_index][:, None]
        )

    def key_tile(side_index, offset):
        return lax.dynamic_index_in_dim(stacks[side_index], offset, 0, keepdims=False)

    def statistic_step(offset, state_pair):
        row_peaks, totals = state_pair
        new_peaks = []
        new_totals = []
        for side_index in range(2):
            allowed = block_mask(side_index, offset)
            current = key_tile(side_index, offset)
            scores = (
                jnp.dot(
                    query_rows[side_index],
                    current[:, :head_width].T,
                    preferred_element_type=jnp.float32,
                )
                * scaling
            )
            masked = jnp.where(allowed, scores, -1e30)
            peak_now = jnp.maximum(row_peaks[side_index], jnp.max(masked, axis=1))
            summed = totals[side_index] * jnp.exp(row_peaks[side_index] - peak_now) + jnp.sum(
                jnp.exp(masked - peak_now[:, None]), axis=1
            )
            peak_now, summed = (peak_now, summed)
            new_peaks.append(peak_now)
            new_totals.append(summed)
        return (jnp.stack(new_peaks), jnp.stack(new_totals))

    start_peaks = jnp.full((2, row_count), -1e30, jnp.float32)
    start_totals = jnp.zeros((2, row_count), jnp.float32)
    row_peaks, totals = lax.fori_loop(0, REACH + 1, statistic_step, (start_peaks, start_totals))
    log_totals = row_peaks + jnp.log(totals)

    def gradient_step(grad_acc, offset):
        query_adds = []
        partials = []
        for side_index in range(2):
            allowed = block_mask(side_index, offset)
            current = key_tile(side_index, offset)
            keys_now = current[:, :head_width]
            values_now = current[:, head_width:]
            scores = (
                jnp.dot(query_rows[side_index], keys_now.T, preferred_element_type=jnp.float32)
                * scaling
            )
            attn_probs = jnp.where(allowed, jnp.exp(scores - log_totals[side_index][:, None]), 0.0)
            probs_low = attn_probs.astype(jnp.bfloat16)
            value_grad = jnp.dot(
                probs_low.T, grad_rows[side_index], preferred_element_type=jnp.float32
            )
            dprobs = jnp.dot(
                grad_rows[side_index], values_now.T, preferred_element_type=jnp.float32
            )
            dscores = (attn_probs * (dprobs - deltas[side_index][:, None])).astype(jnp.bfloat16)
            query_add = jnp.dot(dscores, keys_now, preferred_element_type=jnp.float32)
            key_grad = jnp.dot(
                dscores.T, query_rows[side_index], preferred_element_type=jnp.float32
            )
            query_add, part_now = (query_add, jnp.concatenate([key_grad, value_grad], axis=1))
            query_adds.append(query_add)
            partials.append(part_now)
        return (grad_acc + jnp.stack(query_adds), jnp.stack(partials))

    grad_acc = jnp.zeros((2, row_count, head_width), jnp.float32)
    grad_acc, partials = lax.scan(gradient_step, grad_acc, jnp.arange(REACH + 1, dtype=jnp.int32))

    def retreat(state_pair, offset):
        lower_acc, upper_acc = state_pair
        got_lower = from_behind(lower_acc, "seq", -1)
        got_upper = from_behind(upper_acc, "seq", 1)
        got_lower = jnp.where(device_rank == seq_count - 1, upper_acc, got_lower)
        return ((got_lower + partials[offset, 0], got_upper + partials[offset, 1]), None)

    initial_sums = (partials[REACH, 0], partials[REACH, 1])
    finished, unused_out = lax.scan(
        retreat, initial_sums, jnp.arange(REACH - 1, -1, -1, dtype=jnp.int32)
    )
    lower_sum, upper_sum = finished
    key_sum = jnp.concatenate([lower_sum, upper_sum], axis=0)
    grad_keys = (key_sum[:, :head_width] * scaling).astype(jnp.bfloat16)
    grad_values = key_sum[:, head_width:].astype(jnp.bfloat16)
    grad_queries = (
        (grad_acc * scaling).astype(jnp.bfloat16).reshape(2 * block_rows, head_count * head_width)
    )
    return (grad_queries, grad_keys, grad_values)


def solution(mesh):
    placed = (
        P("seq", "grp"),
        P("seq", "grp"),
        P("seq", "grp"),
        P("seq", "grp"),
        P("seq", "grp"),
        P(),
    )
    return jax.shard_map(
        body,
        mesh=mesh,
        in_specs=placed,
        out_specs=(P("seq", "grp"), P("seq", "grp"), P("seq", "grp")),
        check_vma=False,
    )
```

profile of v0, /device:TPU:0, one launch (start us, length us, event | category | flops | bytes accessed | tf_op | source)
XLA Modules:
  0.0 673.8 jit_solution(15760846539801807998)
XLA Ops:
  2.4 166.8 %while.63 = (s32[]{:T(128)}, bf16[128,256]{1,0:T(8,128)(2,1)S(1)}, bf16[128,256]{1,0:T(8,128)(2,1)S(1)}, bf16[16,128,256]{2,1,0:T(8,128)(2,1)S(1)}, bf16[16,128,...) while((s32[]{:T(128)}, bf16[128,256]{1,0:T(8,128)(2,1)S(1)}, bf16[128,256]{1,0:T(8,128)(2,1)S(1)}, ...), condition=%wide.region_3.4_spmd, body=%wide.region_2.3_spmd.sunk | while | flops 32770 | bytes 1048750 | solution.py:36
  2.4 4.9 collective-permute-start
  9.2 4.3 collective-permute-done.1
  13.5 4.3 collective-permute-start
  19.7 4.3 collective-permute-done.1
  24.0 3.8 collective-permute-start
  29.7 4.3 collective-permute-done.1
  34.0 4.8 collective-permute-start
  40.8 4.3 collective-permute-done.1
  45.1 3.7 collective-permute-start
  50.7 4.6 collective-permute-done.1
  55.4 4.1 collective-permute-start
  61.4 4.7 collective-permute-done.1
  71.7 4.3 collective-permute-done.1
  76.0 4.5 collective-permute-start
  82.4 4.3 collective-permute-done.1
  86.7 4.0 collective-permute-start
  92.6 4.3 collective-permute-done.1
  97.0 4.1 collective-permute-start
  103.0 4.3 collective-permute-done.1
  107.3 3.7 collective-permute-start
  117.2 4.4 collective-permute-start
  123.6 4.8 collective-permute-done.1
  128.5 4.2 collective-permute-start
  134.6 4.6 collective-permute-done.1
  144.7 4.1 collective-permute-done.1
  148.8 4.4 collective-permute-start
  155.1 4.3 collective-permute-done.1
  164.9 4.3 collective-permute-done.1
  173.4 86.6 %while.65 = (s32[]{:T(128)}, f32[2,1024]{1,0:T(2,128)S(1)}, f32[2,1024]{1,0:T(2,128)S(1)}, s32[]{:T(128)}, bf16[17,128,256]{2,1,0:T(8,128)(2,1)}, /*index=5*/bf1...) while((s32[]{:T(128)}, f32[2,1024]{1,0:T(2,128)S(1)}, ...), condition=%wide.region_10.11_spmd.clone.clone, body=%wide.region_5.10_spmd.clone.clone.sunk | while | flops 69216512 | bytes 3166401 | solution.py:99
  260.9 212.3 %while.66 = (s32[]{:T(128)}, f32[2,1024,128]{2,1,0:T(8,128)S(1)}, f32[17,2,128,256]{2,3,1,0:T(8,128)}, s32[17]{0:T(128)S(1)}, s32[]{:T(128)}, /*index=5*/bf16[17...) while((s32[]{:T(128)}, f32[2,1024,128]{2,1,0:T(8,128)S(1)}, ...), condition=%wide.region_13.14_spmd.clone.clone, body=%wide.region_12.13_spmd.clone.clone.sunk | while | flops 339083520 | bytes 12899713 | solution.py:133
  473.2 5.8 copy.20
  480.2 191.2 %while.64 = (s32[]{:T(128)}, f32[128,256]{1,0:T(8,128)S(1)}, f32[128,256]{1,0:T(8,128)S(1)}, pred[]{:T(512)}, s32[16]{0:T(128)S(1)}, /*index=5*/f32[17,2,128,256]{3,2,1,0:T(8,128)}, s32[]{:T(128)}, s32[]{:T(128)}, s32[]{:T(128)}) while((s32[]{:T(128)}, f32[128,256]{1,0:T(8,128)S(1)}, f32[128,256]{1,0:T(8,128)S(1)}, pred[]{:T(512)}, ...), condition=%wide.region_15.16_spmd, body=%wide.region_14.15_spmd.sunk | while | flops 98309 | bytes 1966304 | solution.py:143
  480.2 4.2 collective-permute-start.2
  492.3 4.2 collective-permute-start.2
  504.4 4.0 collective-permute-start.2
  516.3 3.9 collective-permute-start.2
  528.1 4.0 collective-permute-start.2
  540.1 4.4 collective-permute-start.2
  552.4 3.7 collective-permute-start.2
  564.0 3.7 collective-permute-start.2
  575.7 3.9 collective-permute-start.2
  587.5 3.7 collective-permute-start.2
  599.1 4.3 collective-permute-start.2
  607.3 3.8 collective-permute-done.3
  619.2 4.3 collective-permute-done.3
  632.0 4.4 collective-permute-done.3
  658.6 4.8 collective-permute-start.2
  (1090 shorter events, 389.4 us)
Async XLA Ops:
  2.4 6.8 %collective-permute-start = (bf16[128,256]{1,0:T(8,128)(2,1)S(1)}, bf16[128,256]{1,0:T(8,128)(2,1)S(1)}, u32[]{:S(2)}, u32[]{:S(2)}) collective-permute-start(bf16[128,256]{1,0:T(8,128)(2,1)S(1)} %copy.31), channel_id=1, source_target_pairs={{0,2},{2,4},{4,6},{6,8},{8,10},{10,12},{12,14},{14,16},{16,18},{18... | collective-permute-start | bytes 196616 | tf_op jit(solution)/shard_map/while/body/eval_jaxpr/ppermute | solution.py:12
  7.3 6.2 collective-permute-start.1
  13.5 6.2 collective-permute-start
  17.8 6.2 collective-permute-start.1
  27.8 6.2 collective-permute-start.1
  34.0 6.7 collective-permute-start
  38.9 6.2 collective-permute-start.1
  48.8 6.5 collective-permute-start.1
  59.5 6.6 collective-permute-start.1
  69.3 6.7 collective-permute-start.1
  76.0 6.4 collective-permute-start
  107.3 6.2 collective-permute-start
  117.2 6.3 collective-permute-start
  121.7 6.7 collective-permute-start.1
  132.7 6.5 collective-permute-start.1
  142.2 6.5 collective-permute-start.1
  148.8 6.3 collective-permute-start
  480.2 8.0 %collective-permute-start.2 = (f32[128,256]{1,0:T(8,128)S(1)}, f32[128,256]{1,0:T(8,128)S(1)}, u32[]{:S(2)}, u32[]{:S(2)}) collective-permute-start(f32[128,256]{1,0:T(8,128)S(1)} %get-tuple-element.1191), channel_id=1, source_target_pairs={{0,2},{2,4},{4,6},{6,8},{8,10},{10,12},{12,14},{14,16},{16,18},{18... | collective-permute-start | bytes 393224 | tf_op jit(solution)/shard_map/while/body/eval_jaxpr/ppermute | solution.py:12
  484.4 6.9 %collective-permute-start.3 = (f32[128,256]{1,0:T(8,128)S(1)}, f32[128,256]{1,0:T(8,128)S(1)}, u32[]{:S(2)}, u32[]{:S(2)}) collective-permute-start(f32[128,256]{1,0:T(8,128)S(1)} %get-tuple-element.1190), channel_id=1, source_target_pairs={{2,0},{4,2},{6,4},{8,6},{10,8},{12,10},{14,12},{16,14},{18,16},{20... | collective-permute-start | bytes 393224 | tf_op jit(solution)/shard_map/while/body/eval_jaxpr/ppermute | solution.py:12
  492.3 8.0 %collective-permute-start.2 = (f32[128,256]{1,0:T(8,128)S(1)}, f32[128,256]{1,0:T(8,128)S(1)}, u32[]{:S(2)}, u32[]{:S(2)}) collective-permute-start(f32[128,256]{1,0:T(8,128)S(1)} %get-tuple-element.1191), channel_id=1, source_target_pairs={{0,2},{2,4},{4,6},{6,8},{8,10},{10,12},{12,14},{14,16},{16,18},{18... | collective-permute-start | bytes 393224 | tf_op jit(solution)/shard_map/while/body/eval_jaxpr/ppermute | solution.py:12
  496.5 6.9 %collective-permute-start.3 = (f32[128,256]{1,0:T(8,128)S(1)}, f32[128,256]{1,0:T(8,128)S(1)}, u32[]{:S(2)}, u32[]{:S(2)}) collective-permute-start(f32[128,256]{1,0:T(8,128)S(1)} %get-tuple-element.1190), channel_id=1, source_target_pairs={{2,0},{4,2},{6,4},{8,6},{10,8},{12,10},{14,12},{16,14},{18,16},{20... | collective-permute-start | bytes 393224 | tf_op jit(solution)/shard_map/while/body/eval_jaxpr/ppermute | solution.py:12
  504.4 7.8 %collective-permute-start.2 = (f32[128,256]{1,0:T(8,128)S(1)}, f32[128,256]{1,0:T(8,128)S(1)}, u32[]{:S(2)}, u32[]{:S(2)}) collective-permute-start(f32[128,256]{1,0:T(8,128)S(1)} %get-tuple-element.1191), channel_id=1, source_target_pairs={{0,2},{2,4},{4,6},{6,8},{8,10},{10,12},{12,14},{14,16},{16,18},{18... | collective-permute-start | bytes 393224 | tf_op jit(solution)/shard_map/while/body/eval_jaxpr/ppermute | solution.py:12
  508.4 6.9 %collective-permute-start.3 = (f32[128,256]{1,0:T(8,128)S(1)}, f32[128,256]{1,0:T(8,128)S(1)}, u32[]{:S(2)}, u32[]{:S(2)}) collective-permute-start(f32[128,256]{1,0:T(8,128)S(1)} %get-tuple-element.1190), channel_id=1, source_target_pairs={{2,0},{4,2},{6,4},{8,6},{10,8},{12,10},{14,12},{16,14},{18,16},{20... | collective-permute-start | bytes 393224 | tf_op jit(solution)/shard_map/while/body/eval_jaxpr/ppermute | solution.py:12
  516.3 7.7 %collective-permute-start.2 = (f32[128,256]{1,0:T(8,128)S(1)}, f32[128,256]{1,0:T(8,128)S(1)}, u32[]{:S(2)}, u32[]{:S(2)}) collective-permute-start(f32[128,256]{1,0:T(8,128)S(1)} %get-tuple-element.1191), channel_id=1, source_target_pairs={{0,2},{2,4},{4,6},{6,8},{8,10},{10,12},{12,14},{14,16},{16,18},{18... | collective-permute-start | bytes 393224 | tf_op jit(solution)/shard_map/while/body/eval_jaxpr/ppermute | solution.py:12
  520.2 6.9 %collective-permute-start.3 = (f32[128,256]{1,0:T(8,128)S(1)}, f32[128,256]{1,0:T(8,128)S(1)}, u32[]{:S(2)}, u32[]{:S(2)}) collective-permute-start(f32[128,256]{1,0:T(8,128)S(1)} %get-tuple-element.1190), channel_id=1, source_target_pairs={{2,0},{4,2},{6,4},{8,6},{10,8},{12,10},{14,12},{16,14},{18,16},{20... | collective-permute-start | bytes 393224 | tf_op jit(solution)/shard_map/while/body/eval_jaxpr/ppermute | solution.py:12
  528.1 7.9 %collective-permute-start.2 = (f32[128,256]{1,0:T(8,128)S(1)}, f32[128,256]{1,0:T(8,128)S(1)}, u32[]{:S(2)}, u32[]{:S(2)}) collective-permute-start(f32[128,256]{1,0:T(8,128)S(1)} %get-tuple-element.1191), channel_id=1, source_target_pairs={{0,2},{2,4},{4,6},{6,8},{8,10},{10,12},{12,14},{14,16},{16,18},{18... | collective-permute-start | bytes 393224 | tf_op jit(solution)/shard_map/while/body/eval_jaxpr/ppermute | solution.py:12
  532.2 6.9 %collective-permute-start.3 = (f32[128,256]{1,0:T(8,128)S(1)}, f32[128,256]{1,0:T(8,128)S(1)}, u32[]{:S(2)}, u32[]{:S(2)}) collective-permute-start(f32[128,256]{1,0:T(8,128)S(1)} %get-tuple-element.1190), channel_id=1, source_target_pairs={{2,0},{4,2},{6,4},{8,6},{10,8},{12,10},{14,12},{16,14},{18,16},{20... | collective-permute-start | bytes 393224 | tf_op jit(solution)/shard_map/while/body/eval_jaxpr/ppermute | solution.py:12
  540.1 8.3 %collective-permute-start.2 = (f32[128,256]{1,0:T(8,128)S(1)}, f32[128,256]{1,0:T(8,128)S(1)}, u32[]{:S(2)}, u32[]{:S(2)}) collective-permute-start(f32[128,256]{1,0:T(8,128)S(1)} %get-tuple-element.1191), channel_id=1, source_target_pairs={{0,2},{2,4},{4,6},{6,8},{8,10},{10,12},{12,14},{14,16},{16,18},{18... | collective-permute-start | bytes 393224 | tf_op jit(solution)/shard_map/while/body/eval_jaxpr/ppermute | solution.py:12
  544.5 6.9 %collective-permute-start.3 = (f32[128,256]{1,0:T(8,128)S(1)}, f32[128,256]{1,0:T(8,128)S(1)}, u32[]{:S(2)}, u32[]{:S(2)}) collective-permute-start(f32[128,256]{1,0:T(8,128)S(1)} %get-tuple-element.1190), channel_id=1, source_target_pairs={{2,0},{4,2},{6,4},{8,6},{10,8},{12,10},{14,12},{16,14},{18,16},{20... | collective-permute-start | bytes 393224 | tf_op jit(solution)/shard_map/while/body/eval_jaxpr/ppermute | solution.py:12
  552.4 7.6 %collective-permute-start.2 = (f32[128,256]{1,0:T(8,128)S(1)}, f32[128,256]{1,0:T(8,128)S(1)}, u32[]{:S(2)}, u32[]{:S(2)}) collective-permute-start(f32[128,256]{1,0:T(8,128)S(1)} %get-tuple-element.1191), channel_id=1, source_target_pairs={{0,2},{2,4},{4,6},{6,8},{8,10},{10,12},{12,14},{14,16},{16,18},{18... | collective-permute-start | bytes 393224 | tf_op jit(solution)/shard_map/while/body/eval_jaxpr/ppermute | solution.py:12
  556.1 6.9 %collective-permute-start.3 = (f32[128,256]{1,0:T(8,128)S(1)}, f32[128,256]{1,0:T(8,128)S(1)}, u32[]{:S(2)}, u32[]{:S(2)}) collective-permute-start(f32[128,256]{1,0:T(8,128)S(1)} %get-tuple-element.1190), channel_id=1, source_target_pairs={{2,0},{4,2},{6,4},{8,6},{10,8},{12,10},{14,12},{16,14},{18,16},{20... | collective-permute-start | bytes 393224 | tf_op jit(solution)/shard_map/while/body/eval_jaxpr/ppermute | solution.py:12
  564.0 7.6 %collective-permute-start.2 = (f32[128,256]{1,0:T(8,128)S(1)}, f32[128,256]{1,0:T(8,128)S(1)}, u32[]{:S(2)}, u32[]{:S(2)}) collective-permute-start(f32[128,256]{1,0:T(8,128)S(1)} %get-tuple-element.1191), channel_id=1, source_target_pairs={{0,2},{2,4},{4,6},{6,8},{8,10},{10,12},{12,14},{14,16},{16,18},{18... | collective-permute-start | bytes 393224 | tf_op jit(solution)/shard_map/while/body/eval_jaxpr/ppermute | solution.py:12
  567.8 6.9 %collective-permute-start.3 = (f32[128,256]{1,0:T(8,128)S(1)}, f32[128,256]{1,0:T(8,128)S(1)}, u32[]{:S(2)}, u32[]{:S(2)}) collective-permute-start(f32[128,256]{1,0:T(8,128)S(1)} %get-tuple-element.1190), channel_id=1, source_target_pairs={{2,0},{4,2},{6,4},{8,6},{10,8},{12,10},{14,12},{16,14},{18,16},{20... | collective-permute-start | bytes 393224 | tf_op jit(solution)/shard_map/while/body/eval_jaxpr/ppermute | solution.py:12
  575.7 7.7 %collective-permute-start.2 = (f32[128,256]{1,0:T(8,128)S(1)}, f32[128,256]{1,0:T(8,128)S(1)}, u32[]{:S(2)}, u32[]{:S(2)}) collective-permute-start(f32[128,256]{1,0:T(8,128)S(1)} %get-tuple-element.1191), channel_id=1, source_target_pairs={{0,2},{2,4},{4,6},{6,8},{8,10},{10,12},{12,14},{14,16},{16,18},{18... | collective-permute-start | bytes 393224 | tf_op jit(solution)/shard_map/while/body/eval_jaxpr/ppermute | solution.py:12
  579.6 6.9 %collective-permute-start.3 = (f32[128,256]{1,0:T(8,128)S(1)}, f32[128,256]{1,0:T(8,128)S(1)}, u32[]{:S(2)}, u32[]{:S(2)}) collective-permute-start(f32[128,256]{1,0:T(8,128)S(1)} %get-tuple-element.1190), channel_id=1, source_target_pairs={{2,0},{4,2},{6,4},{8,6},{10,8},{12,10},{14,12},{16,14},{18,16},{20... | collective-permute-start | bytes 393224 | tf_op jit(solution)/shard_map/while/body/eval_jaxpr/ppermute | solution.py:12
  587.5 7.6 %collective-permute-start.2 = (f32[128,256]{1,0:T(8,128)S(1)}, f32[128,256]{1,0:T(8,128)S(1)}, u32[]{:S(2)}, u32[]{:S(2)}) collective-permute-start(f32[128,256]{1,0:T(8,128)S(1)} %get-tuple-element.1191), channel_id=1, source_target_pairs={{0,2},{2,4},{4,6},{6,8},{8,10},{10,12},{12,14},{14,16},{16,18},{18... | collective-permute-start | bytes 393224 | tf_op jit(solution)/shard_map/while/body/eval_jaxpr/ppermute | solution.py:12
  591.2 6.9 %collective-permute-start.3 = (f32[128,256]{1,0:T(8,128)S(1)}, f32[128,256]{1,0:T(8,128)S(1)}, u32[]{:S(2)}, u32[]{:S(2)}) collective-permute-start(f32[128,256]{1,0:T(8,128)S(1)} %get-tuple-element.1190), channel_id=1, source_target_pairs={{2,0},{4,2},{6,4},{8,6},{10,8},{12,10},{14,12},{16,14},{18,16},{20... | collective-permute-start | bytes 393224 | tf_op jit(solution)/shard_map/while/body/eval_jaxpr/ppermute | solution.py:12
  599.1 8.1 %collective-permute-start.2 = (f32[128,256]{1,0:T(8,128)S(1)}, f32[128,256]{1,0:T(8,128)S(1)}, u32[]{:S(2)}, u32[]{:S(2)}) collective-permute-start(f32[128,256]{1,0:T(8,128)S(1)} %get-tuple-element.1191), channel_id=1, source_target_pairs={{0,2},{2,4},{4,6},{6,8},{8,10},{10,12},{12,14},{14,16},{16,18},{18... | collective-permute-start | bytes 393224 | tf_op jit(solution)/shard_map/while/body/eval_jaxpr/ppermute | solution.py:12
  603.4 7.7 %collective-permute-start.3 = (f32[128,256]{1,0:T(8,128)S(1)}, f32[128,256]{1,0:T(8,128)S(1)}, u32[]{:S(2)}, u32[]{:S(2)}) collective-permute-start(f32[128,256]{1,0:T(8,128)S(1)} %get-tuple-element.1190), channel_id=1, source_target_pairs={{2,0},{4,2},{6,4},{8,6},{10,8},{12,10},{14,12},{16,14},{18,16},{20... | collective-permute-start | bytes 393224 | tf_op jit(solution)/shard_map/while/body/eval_jaxpr/ppermute | solution.py:12
  612.1 7.1 %collective-permute-start.2 = (f32[128,256]{1,0:T(8,128)S(1)}, f32[128,256]{1,0:T(8,128)S(1)}, u32[]{:S(2)}, u32[]{:S(2)}) collective-permute-start(f32[128,256]{1,0:T(8,128)S(1)} %get-tuple-element.1191), channel_id=1, source_target_pairs={{0,2},{2,4},{4,6},{6,8},{8,10},{10,12},{12,14},{14,16},{16,18},{18... | collective-permute-start | bytes 393224 | tf_op jit(solution)/shard_map/while/body/eval_jaxpr/ppermute | solution.py:12
  615.4 8.1 %collective-permute-start.3 = (f32[128,256]{1,0:T(8,128)S(1)}, f32[128,256]{1,0:T(8,128)S(1)}, u32[]{:S(2)}, u32[]{:S(2)}) collective-permute-start(f32[128,256]{1,0:T(8,128)S(1)} %get-tuple-element.1190), channel_id=1, source_target_pairs={{2,0},{4,2},{6,4},{8,6},{10,8},{12,10},{14,12},{16,14},{18,16},{20... | collective-permute-start | bytes 393224 | tf_op jit(solution)/shard_map/while/body/eval_jaxpr/ppermute | solution.py:12
  624.6 7.4 %collective-permute-start.2 = (f32[128,256]{1,0:T(8,128)S(1)}, f32[128,256]{1,0:T(8,128)S(1)}, u32[]{:S(2)}, u32[]{:S(2)}) collective-permute-start(f32[128,256]{1,0:T(8,128)S(1)} %get-tuple-element.1191), channel_id=1, source_target_pairs={{0,2},{2,4},{4,6},{6,8},{8,10},{10,12},{12,14},{14,16},{16,18},{18... | collective-permute-start | bytes 393224 | tf_op jit(solution)/shard_map/while/body/eval_jaxpr/ppermute | solution.py:12
  628.1 8.2 %collective-permute-start.3 = (f32[128,256]{1,0:T(8,128)S(1)}, f32[128,256]{1,0:T(8,128)S(1)}, u32[]{:S(2)}, u32[]{:S(2)}) collective-permute-start(f32[128,256]{1,0:T(8,128)S(1)} %get-tuple-element.1190), channel_id=1, source_target_pairs={{2,0},{4,2},{6,4},{8,6},{10,8},{12,10},{14,12},{16,14},{18,16},{20... | collective-permute-start | bytes 393224 | tf_op jit(solution)/shard_map/while/body/eval_jaxpr/ppermute | solution.py:12
  639.5 6.9 %collective-permute-start.3 = (f32[128,256]{1,0:T(8,128)S(1)}, f32[128,256]{1,0:T(8,128)S(1)}, u32[]{:S(2)}, u32[]{:S(2)}) collective-permute-start(f32[128,256]{1,0:T(8,128)S(1)} %get-tuple-element.1190), channel_id=1, source_target_pairs={{2,0},{4,2},{6,4},{8,6},{10,8},{12,10},{14,12},{16,14},{18,16},{20... | collective-permute-start | bytes 393224 | tf_op jit(solution)/shard_map/while/body/eval_jaxpr/ppermute | solution.py:12
  647.4 7.2 %collective-permute-start.2 = (f32[128,256]{1,0:T(8,128)S(1)}, f32[128,256]{1,0:T(8,128)S(1)}, u32[]{:S(2)}, u32[]{:S(2)}) collective-permute-start(f32[128,256]{1,0:T(8,128)S(1)} %get-tuple-element.1191), channel_id=1, source_target_pairs={{0,2},{2,4},{4,6},{6,8},{8,10},{10,12},{12,14},{14,16},{16,18},{18... | collective-permute-start | bytes 393224 | tf_op jit(solution)/shard_map/while/body/eval_jaxpr/ppermute | solution.py:12
  650.7 6.9 %collective-permute-start.3 = (f32[128,256]{1,0:T(8,128)S(1)}, f32[128,256]{1,0:T(8,128)S(1)}, u32[]{:S(2)}, u32[]{:S(2)}) collective-permute-start(f32[128,256]{1,0:T(8,128)S(1)} %get-tuple-element.1190), channel_id=1, source_target_pairs={{2,0},{4,2},{6,4},{8,6},{10,8},{12,10},{14,12},{16,14},{18,16},{20... | collective-permute-start | bytes 393224 | tf_op jit(solution)/shard_map/while/body/eval_jaxpr/ppermute | solution.py:12
  658.6 8.7 %collective-permute-start.2 = (f32[128,256]{1,0:T(8,128)S(1)}, f32[128,256]{1,0:T(8,128)S(1)}, u32[]{:S(2)}, u32[]{:S(2)}) collective-permute-start(f32[128,256]{1,0:T(8,128)S(1)} %get-tuple-element.1191), channel_id=1, source_target_pairs={{0,2},{2,4},{4,6},{6,8},{8,10},{10,12},{12,14},{14,16},{16,18},{18... | collective-permute-start | bytes 393224 | tf_op jit(solution)/shard_map/while/body/eval_jaxpr/ppermute | solution.py:12
  663.5 6.9 %collective-permute-start.3 = (f32[128,256]{1,0:T(8,128)S(1)}, f32[128,256]{1,0:T(8,128)S(1)}, u32[]{:S(2)}, u32[]{:S(2)}) collective-permute-start(f32[128,256]{1,0:T(8,128)S(1)} %get-tuple-element.1190), channel_id=1, source_target_pairs={{2,0},{4,2},{6,4},{8,6},{10,8},{12,10},{14,12},{16,14},{18,16},{20... | collective-permute-start | bytes 393224 | tf_op jit(solution)/shard_map/while/body/eval_jaxpr/ppermute | solution.py:12
  (54 other events, 331.0 us)
where the time goes:
time: 680 us; the launch traced here: 674 us
  local copies, waits for them, and re-layouts  179 us (26%)
  starting transfers between devices  167 us (25%)
  waiting for transfers between devices  132 us (19%)
  loops' own time  96 us (14%)
  matrix products  54.7 us (8%)
  other arithmetic  44.4 us (7%)
    ppermute x64, starting transfers between devices, from_behind(): return lax.ppermute(shard, axis, pairs)  167 us
    ppermute x64, waiting for transfers between devices, from_behind(): return lax.ppermute(shard, axis, pairs)  132 us
    another operation x1, loops' own time, body(): lax.scan(gradient_step, grad_acc, jnp.arange(REACH + 1, dtype=jnp.int32))  61.3 us
    broadcast_in_dim x68, local copies, waits for them, and re-layouts, body(): jnp.repeat(jnp.max(jnp.where(doc_starts[None, :] <= block_pos[:, None], d...  49.1 us
    broadcast_in_dim x68, local copies, waits for them, and re-layouts, body(): query_pos.append(jnp.repeat(block_pos, head_count))  48.6 us
    another operation x1, loops' own time, body(): lax.scan(retreat, initial_sums, jnp.arange(REACH - 1, -1, -1, dtype=jnp.i...  31.7 us
    squeeze x34, local copies, waits for them, and re-layouts, key_tile(): lax.dynamic_index_in_dim(stacks[side_index], offset, 0, keepdims=False)  30.2 us
    add x16, other arithmetic, retreat(): got_upper + partials[offset, 1]  16.5 us
  transfers between devices with their start and end apart: 64, of which 49 were waited for; matrix products, arithmetic and copies ran while one was open for 1% of the time, Pallas kernels for 0%

commit v1 on v0

v1 whole, which is shorter than its diff:
```python
import functools

import jax
import jax.numpy as jnp
from jax import lax
from jax.experimental import pallas as pl
from jax.experimental.pallas import tpu as pltpu
from jax.sharding import PartitionSpec as P

REACH = 16


def _bwd_kernel(blk_ref, kb0_ref, q_ref, do_ref, kv_ref, kt_ref, begin_ref, qpos_ref,
                delta_ref, dq_ref, dkv_ref, qall, doall, dqt,
                *, rows, heads, width, reach, scaling):
    s = pl.program_id(0)
    b = blk_ref[s]
    kb0 = kb0_ref[s]
    for h in range(heads):
        qall[h * rows:(h + 1) * rows, :] = q_ref[:, h * width:(h + 1) * width]
        doall[h * rows:(h + 1) * rows, :] = do_ref[:, h * width:(h + 1) * width]
    begin = begin_ref[...]
    qpos = qpos_ref[...]
    delta = delta_ref[...]
    dqt[...] = jnp.zeros(dqt.shape, jnp.float32)
    dkv_ref[...] = jnp.zeros(dkv_ref.shape, jnp.float32)
    k_iota = lax.broadcasted_iota(jnp.int32, (rows, 1), 0)
    base = (b - reach) * rows
    nt = (((1,), (1,)), ((), ()))

    def scores(c):
        kc = kv_ref[c, :, :width]
        st = lax.dot_general(kc, qall[...], nt, preferred_element_type=jnp.float32) * scaling
        kpos = base + c * rows + k_iota
        allowed = (kpos >= begin) & (kpos <= qpos)
        return st, allowed

    def stat_step(c, carry):
        m, l = carry
        st, allowed = scores(c)
        masked = jnp.where(allowed, st, -1e30)
        m_new = jnp.maximum(m, jnp.max(masked, axis=0, keepdims=True))
        e = jnp.where(allowed, jnp.exp(st - m_new), 0.0)
        l = l * jnp.exp(m - m_new) + jnp.sum(e, axis=0, keepdims=True)
        return m_new, l

    cols = heads * rows
    m0 = jnp.full((1, cols), -1e30, jnp.float32)
    l0 = jnp.zeros((1, cols), jnp.float32)
    m, l = lax.fori_loop(kb0, reach + 1, stat_step, (m0, l0))
    lse = m + jnp.log(l)

    def grad_step(c, carry):
        st, allowed = scores(c)
        p = jnp.where(allowed, jnp.exp(st - lse), 0.0)
        vc = kv_ref[c, :, width:]
        dpt = lax.dot_general(vc, doall[...], nt, preferred_element_type=jnp.float32)
        ds = (p * (dpt - delta)).astype(jnp.bfloat16)
        pb = p.astype(jnp.bfloat16)
        dk = jnp.dot(ds, qall[...], preferred_element_type=jnp.float32) * scaling
        dv = jnp.dot(pb, doall[...], preferred_element_type=jnp.float32)
        dkv_ref[c, :, :width] = dk
        dkv_ref[c, :, width:] = dv
        dqt[...] += jnp.dot(kt_ref[c], ds, preferred_element_type=jnp.float32)
        return carry

    lax.fori_loop(kb0, reach + 1, grad_step, 0)
    for h in range(heads):
        piece = dqt[:, h * rows:(h + 1) * rows]
        dq_ref[:, h * width:(h + 1) * width] = (piece.T * scaling).astype(jnp.bfloat16)


def body(queries, shared_keys, shared_values, outputs, out_grad, doc_lengths):
    rank = lax.axis_index("seq")
    n_seq = lax.axis_size("seq")
    rows = shared_keys.shape[0] // 2
    width = shared_keys.shape[1]
    heads = queries.shape[1] // width
    scaling = width ** (-0.5)
    win = REACH + 1
    doc_ends = jnp.cumsum(doc_lengths)
    doc_starts = doc_ends - doc_lengths
    blocks = jnp.stack([rank, 2 * n_seq - 1 - rank]).astype(jnp.int32)

    kv_local = jnp.concatenate([shared_keys, shared_values], axis=1)
    kv_all = lax.all_gather(kv_local, "seq", axis=0, tiled=True)
    kv_st = kv_all.reshape(n_seq, 2, rows, 2 * width)
    kv_seq = jnp.concatenate(
        [jnp.zeros((REACH, rows, 2 * width), kv_all.dtype), kv_st[:, 0], kv_st[::-1, 1]], axis=0
    )
    windows = jnp.stack(
        [lax.dynamic_slice_in_dim(kv_seq, blocks[i], win, 0) for i in range(2)]
    )
    kt = jnp.swapaxes(windows[..., :width], 2, 3)

    base_pos = jnp.arange(rows, dtype=jnp.int32)
    pos = blocks[:, None] * rows + base_pos[None, :]
    begins = jnp.max(
        jnp.where(doc_starts[None, None, :] <= pos[:, :, None], doc_starts[None, None, :], 0), axis=2
    ).astype(jnp.int32)
    kb0 = jnp.maximum(0, begins[:, 0] // rows - (blocks - REACH)).astype(jnp.int32)
    begin_t = jnp.tile(begins, (1, heads)).reshape(2, 1, heads * rows)
    qpos_t = jnp.tile(pos, (1, heads)).reshape(2, 1, heads * rows)
    prod = out_grad.astype(jnp.float32) * outputs.astype(jnp.float32)
    deltas = jnp.sum(prod.reshape(2, rows, heads, width), axis=3)
    delta_t = jnp.swapaxes(deltas, 1, 2).reshape(2, 1, heads * rows)

    kernel = functools.partial(
        _bwd_kernel, rows=rows, heads=heads, width=width, reach=REACH, scaling=scaling
    )
    cols = heads * rows
    grid_spec = pltpu.PrefetchScalarGridSpec(
        num_scalar_prefetch=2,
        grid=(2,),
        in_specs=[
            pl.BlockSpec((rows, cols), lambda s, blk, k0: (s, 0)),
            pl.BlockSpec((rows, cols), lambda s, blk, k0: (s, 0)),
            pl.BlockSpec((None, win, rows, 2 * width), lambda s, blk, k0: (s, 0, 0, 0)),
            pl.BlockSpec((None, win, width, rows), lambda s, blk, k0: (s, 0, 0, 0)),
            pl.BlockSpec((None, 1, cols), lambda s, blk, k0: (s, 0, 0)),
            pl.BlockSpec((None, 1, cols), lambda s, blk, k0: (s, 0, 0)),
            pl.BlockSpec((None, 1, cols), lambda s, blk, k0: (s, 0, 0)),
        ],
        out_specs=[
            pl.BlockSpec((rows, cols), lambda s, blk, k0: (s, 0)),
            pl.BlockSpec((None, win, rows, 2 * width), lambda s, blk, k0: (s, 0, 0, 0)),
        ],
        scratch_shapes=[
            pltpu.VMEM((cols, width), jnp.bfloat16),
            pltpu.VMEM((cols, width), jnp.bfloat16),
            pltpu.VMEM((width, cols), jnp.float32),
        ],
    )
    flops = 2 * 2 * win * 6 * rows * cols * width
    grad_queries, partial = pl.pallas_call(
        kernel,
        grid_spec=grid_spec,
        out_shape=[
            jax.ShapeDtypeStruct((2 * rows, cols), jnp.bfloat16),
            jax.ShapeDtypeStruct((2, win, rows, 2 * width), jnp.float32),
        ],
        compiler_params=pltpu.CompilerParams(dimension_semantics=("arbitrary",)),
        cost_estimate=pl.CostEstimate(
            flops=flops, transcendentals=2 * 2 * win * rows * cols, bytes_accessed=8 << 20
        ),
    )(blocks, kb0, queries, out_grad, windows, kt, begin_t, qpos_t, delta_t)

    acc = jnp.zeros((2 * n_seq + REACH, rows, 2 * width), jnp.float32)
    acc = lax.dynamic_update_slice_in_dim(acc, partial[0], blocks[0], 0)
    cur = lax.dynamic_slice_in_dim(acc, blocks[1], win, 0)
    acc = lax.dynamic_update_slice_in_dim(acc, cur + partial[1], blocks[1], 0)
    acc = acc[REACH:]
    storage = jnp.stack([acc[:n_seq], acc[n_seq:][::-1]], axis=1).reshape(2 * n_seq * rows, 2 * width)
    summed = lax.psum_scatter(storage, "seq", scatter_dimension=0, tiled=True)
    grad_keys = summed[:, :width].astype(jnp.bfloat16)
    grad_values = summed[:, width:].astype(jnp.bfloat16)
    return (grad_queries, grad_keys, grad_values)


def solution(mesh):
    placed = (
        P("seq", "grp"),
        P("seq", "grp"),
        P("seq", "grp"),
        P("seq", "grp"),
        P("seq", "grp"),
        P(),
    )
    return jax.shard_map(
        body,
        mesh=mesh,
        in_specs=placed,
        out_specs=(P("seq", "grp"), P("seq", "grp"), P("seq", "grp")),
        check_vma=False,
    )
```

time: 680 us -> 216 us (0.32)
  starting transfers between devices: 167 us -> 0.08 us
  local copies, waits for them, and re-layouts: 179 us -> 14.9 us
  loops' own time: 96 us -> 0 us
  matrix products: 54.7 us -> 0 us
  waiting for transfers between devices: 132 us -> 171 us
  other arithmetic: 44.4 us -> 8.35 us
  between operations: 0.87 us -> 14.2 us
  Pallas kernels: 0 us -> 7.75 us
    ppermute x64 -> x0, starting transfers between devices: 167 us -> none  [from_behind(): return lax.ppermute(shard, axis, pairs)]
    ppermute x64 -> x0, waiting for transfers between devices: 132 us -> none  [from_behind(): return lax.ppermute(shard, axis, pairs)]
    reduce_scatter x0 -> x1, waiting for transfers between devices: none -> 110 us  [body(): summed = lax.psum_scatter(storage, 'seq', scatter_dimension=0, tiled=True)]
    broadcast_in_dim x139 -> x2, local copies, waits for them, and re-layouts: 97.8 us -> 0.73 us  [the longest x1 0.73 us: body(): acc = jnp.zeros((2 * n_seq + REACH, rows, 2 * width), jnp.float32)]
    another operation x4 -> x0, loops' own time: 96 us -> none  [the longest x1 61.3 us: body(): lax.scan(gradient_step, grad_acc, jnp.arange(REACH + 1, dtype=jnp.int32))]
    all_gather x0 -> x1, waiting for transfers between devices: none -> 60.5 us  [body(): kv_all = lax.all_gather(kv_local, 'seq', axis=0, tiled=True)]
    dot_general x204 -> x0, matrix products: 54.7 us -> none  [the longest x34 10.1 us: gradient_step(): jnp.dot(query_rows[side_index], keys_now.T, preferred_element_type=jnp.fl...]
    squeeze x35 -> x1, local copies, waits for them, and re-layouts: 31.2 us -> 0.07 us  [body(): kv_st[::-1, 1]]
  transfers between devices with their start and end apart: 64 -> 2, of which waited for: 49 -> 2; matrix products, arithmetic and copies ran while one was open for 1% -> 2% of each run, Pallas kernels for 0% -> 0%
where the time goes in v1:
time: 216 us
  waiting for transfers between devices  171 us (79%)
  local copies, waits for them, and re-layouts  14.9 us (7%)
  between operations  14.2 us (7%)
  other arithmetic  8.35 us (4%)
  Pallas kernels  7.75 us (4%)
    reduce_scatter x1, waiting for transfers between devices, body(): summed = lax.psum_scatter(storage, 'seq', scatter_dimension=0, tiled=True)  110 us
    all_gather x1, waiting for transfers between devices, body(): kv_all = lax.all_gather(kv_local, 'seq', axis=0, tiled=True)  60.5 us
    pallas_call x1, Pallas kernels, body(): pl.pallas_call(kernel, grid_spec=grid_spec, out_shape=[jax.ShapeDtypeStru...  7.75 us
  transfers between devices with their start and end apart: 2, of which 2 were waited for; matrix products, arithmetic and copies ran while one was open for 2% of the time, Pallas kernels for 0%

profile of v1, /device:TPU:0, one launch (start us, length us, event | category | flops | bytes accessed | tf_op | source)
XLA Modules:
  0.0 216.1 jit_solution(13868786951561825465)
XLA Ops:
  7.2 0.0 all-gather.2.cloned.1.call-start
  7.2 1.5 pad_maximum_fusion.3
  8.8 0.0 all-gather.2.cloned.1.call-update
  8.8 0.0 reduce-scatter.2.cloned.1.call-start
  8.8 0.7 copy.33
  9.6 0.1 reduce-window.9
  9.7 0.1 reduce
  9.8 0.7 sub.17
  10.5 1.4 multiply_bitcast_fusion
  11.8 0.2 copy.41
  12.0 0.3 bitcast_reduce_fusion
  12.4 0.7 copy.36
  13.1 0.1 broadcast_multiply_fusion
  13.1 0.0 copy-start.1
  13.1 0.1 iota_add_fusion
  13.2 0.1 select_reduce_fusion
  13.3 0.1 slice_reduce_fusion
  13.4 0.6 subtract_maximum_fusion.kb0_ref
  14.0 60.5 %all-gather.2.cloned.1.call-done = bf16[4096,256]{1,0:T(8,128)(2,1)} async-done(((bf16[256,256]{1,0:T(8,128)(2,1)}), bf16[4096,256]{1,0:T(8,128)(2,1)}) %all-gather.2.cloned.1.call-update) | async-done | bytes 2097168 | tf_op jit(solution)/shard_map/all_gather | solution.py:86
  74.5 1.7 fusion.3
  76.1 0.7 copy.39
  76.8 0.0 copy-done.1
  76.8 0.7 copy.40
  77.5 0.1 reverse_bitcast_fusion.1
  77.6 0.3 pad_maximum_fusion.1
  77.9 0.2 dynamic-slice_bitcast_fusion.1
  78.0 1.1 fusion.2.kt_ref
  79.1 0.2 pad_maximum_fusion.2
  79.3 2.7 %copy.37.kv_ref = bf16[2,17,128,256]{3,2,1,0:T(8,128)(2,1)} copy(bf16[2,17,128,256]{2,3,1,0:T(8,128)(2,1)S(1)} %pad_maximum_fusion.2) | data formatting | bytes 4456448 | tf_op jit(solution)/shard_map/stack | solution.py:91
  82.0 0.6 tile.18
  82.6 0.6 tile.16
  83.2 7.7 %shard_map.85 = (bf16[256,1024]{1,0:T(8,128)(2,1)}, f32[2,17,128,256]{3,2,1,0:T(8,128)}) custom-call(s32[2]{0:T(128)} %copy-done.1, s32[2]{0:T(128)} %subtract_maximum_fusion.kb0_ref, bf16[256,1024]{1,0:T(8,128)(2,1)} %q_ref.1, bf16[256,1024]{1,0:T(8,128)(2,1)} %do_ref.1, bf16[2,17,128,256]{3,2,1,0:T(8,128)(2,1)} %copy.37.kv_ref, ...), custom_call_target="tpu_custom_call" | custom-call | flops 6845104128 | bytes 8388608 | tf_op jit(solution)/shard_map/pallas_call | solution.py:135
  91.0 0.0 copy-start
  91.0 0.7 broadcast_in_dim.23
  91.7 1.5 copy-done
  93.2 0.2 bitcast_dynamic-update-slice_fusion
  93.4 0.4 fusion
  93.9 0.4 slice_bitcast_fusion
  94.3 0.2 reverse_bitcast_fusion
  94.5 0.4 pad_maximum_fusion
  95.0 2.3 %copy.38 = f32[16,2,128,256]{3,2,1,0:T(8,128)} copy(f32[16,2,128,256]{3,2,0,1:T(8,128)S(1)} %pad_maximum_fusion) | data formatting | bytes 8388608 | tf_op jit(solution)/shard_map/stack | solution.py:153
  97.2 0.0 reduce-scatter.2.cloned.1.call-update
  97.3 110.4 %reduce-scatter.2.cloned.1.call-done = f32[256,256]{1,0:T(8,128)} async-done(((f32[4096,256]{1,0:T(8,128)}), f32[256,256]{1,0:T(8,128)}) %reduce-scatter.2.cloned.1.call-update) | async-done | bytes 262160 | tf_op jit(solution)/shard_map/reduce_scatter | solution.py:154
  207.6 1.0 convert.4
  208.6 0.7 fusion.4
  (2 shorter events, 0.0 us)
Async XLA Ops:
  7.2 67.3 %all-gather.2.cloned.1.call-start = ((), (), s32[]{:S(2)}) async-start(), calls=%async_computation.1 | async-start | bytes 2228224 | tf_op jit(solution)/shard_map/all_gather | solution.py:86
  8.8 198.9 %reduce-scatter.2.cloned.1.call-start = ((), (), s32[]{:S(2)}) async-start(), calls=%async_computation.2 | async-start | bytes 4456448 | tf_op jit(solution)/shard_map/reduce_scatter | solution.py:154
  13.1 63.7 %copy-start.1 = (s32[2]{0:T(128)}, s32[2]{0:T(128)S(1)}, u32[]{:S(2)}) copy-start(s32[2]{0:T(128)S(1)} %get-tuple-element.8.blk_ref) | copy-start | bytes 28
  91.0 2.3 %copy-start = (f32[2,17,128,256]{3,2,1,0:T(8,128)S(1)}, f32[2,17,128,256]{3,2,1,0:T(8,128)}, u32[]{:S(2)}) copy-start(f32[2,17,128,256]{3,2,1,0:T(8,128)} %get-tuple-element.6) | copy-start | bytes 13369348
Sparse Core Ops, SparseCore 0:
  11.3 63.0 all-gather.1
  97.4 110.1 reduce-scatter.1

commit v2 on v1

--- a/solution.py
+++ b/solution.py
@@ -83,7 +83,8 @@
     blocks = jnp.stack([rank, 2 * n_seq - 1 - rank]).astype(jnp.int32)
 
     kv_local = jnp.concatenate([shared_keys, shared_values], axis=1)
-    kv_all = lax.all_gather(kv_local, "seq", axis=0, tiled=True)
+    kv_rep = jnp.broadcast_to(kv_local[None], (n_seq,) + kv_local.shape)
+    kv_all = lax.all_to_all(kv_rep, "seq", 0, 0)
     kv_st = kv_all.reshape(n_seq, 2, rows, 2 * width)
     kv_seq = jnp.concatenate(
         [jnp.zeros((REACH, rows, 2 * width), kv_all.dtype), kv_st[:, 0], kv_st[::-1, 1]], axis=0
@@ -150,8 +151,9 @@
     cur = lax.dynamic_slice_in_dim(acc, blocks[1], win, 0)
     acc = lax.dynamic_update_slice_in_dim(acc, cur + partial[1], blocks[1], 0)
     acc = acc[REACH:]
-    storage = jnp.stack([acc[:n_seq], acc[n_seq:][::-1]], axis=1).reshape(2 * n_seq * rows, 2 * width)
-    summed = lax.psum_scatter(storage, "seq", scatter_dimension=0, tiled=True)
+    storage = jnp.stack([acc[:n_seq], acc[n_seq:][::-1]], axis=1)
+    received = lax.all_to_all(storage, "seq", 0, 0)
+    summed = jnp.sum(received, axis=0).reshape(2 * rows, 2 * width)
     grad_keys = summed[:, :width].astype(jnp.bfloat16)
     grad_values = summed[:, width:].astype(jnp.bfloat16)
     return (grad_queries, grad_keys, grad_values)

time: 216 us -> 198 us (0.917)
  waiting for transfers between devices: 171 us -> 40.4 us
  blocking collectives: 0 us -> 117 us
  between operations: 14.2 us -> 0.83 us
  starting transfers between devices: 0.08 us -> 8.47 us
    all_to_all x0 -> x1, blocking collectives: none -> 117 us  [body(): received = lax.all_to_all(storage, 'seq', 0, 0)]
    reduce_scatter x1 -> x0, waiting for transfers between devices: 110 us -> none  [body(): summed = lax.psum_scatter(storage, 'seq', scatter_dimension=0, tiled=True)]
    all_gather x1 -> x0, waiting for transfers between devices: 60.5 us -> none  [body(): kv_all = lax.all_gather(kv_local, 'seq', axis=0, tiled=True)]
    all_to_all x0 -> x1, waiting for transfers between devices: none -> 40.4 us  [body(): kv_all = lax.all_to_all(kv_rep, 'seq', 0, 0)]
    all_to_all x0 -> x1, starting transfers between devices: none -> 8.47 us  [body(): kv_all = lax.all_to_all(kv_rep, 'seq', 0, 0)]
    another operation x4, local copies, waits for them, and re-layouts: 3.65 us -> 1.17 us  [the longest x3 1.08 us: body(): storage = jnp.stack([acc[:n_seq], acc[n_seq:][::-1]], axis=1)]
    reduce_sum x0 -> x1, other arithmetic: none -> 2.46 us  [body(): summed = jnp.sum(received, axis=0).reshape(2 * rows, 2 * width)]
  transfers between devices with their start and end apart: 2 -> 1, of which waited for: 2 -> 1; matrix products, arithmetic and copies ran while one was open for 2% -> 1% of each run, Pallas kernels for 0% -> 0%
where the time goes in v2:
time: 198 us
  blocking collectives  117 us (59%)
  waiting for transfers between devices  40.4 us (20%)
  local copies, waits for them, and re-layouts  14.3 us (7%)
  other arithmetic  8.72 us (4%)
  starting transfers between devices  8.47 us (4%)
  Pallas kernels  7.75 us (4%)
    all_to_all x1, blocking collectives, body(): received = lax.all_to_all(storage, 'seq', 0, 0)  117 us
    all_to_all x1, waiting for transfers between devices, body(): kv_all = lax.all_to_all(kv_rep, 'seq', 0, 0)  40.4 us
    all_to_all x1, starting transfers between devices, body(): kv_all = lax.all_to_all(kv_rep, 'seq', 0, 0)  8.47 us
    pallas_call x1, Pallas kernels, body(): pl.pallas_call(kernel, grid_spec=grid_spec, out_shape=[jax.ShapeDtypeStru...  7.75 us
    another operation x1, local copies, waits for them, and re-layouts, body(): jnp.stack([lax.dynamic_slice_in_dim(kv_seq, blocks[i], win, 0) for i in r...  4.14 us
  transfers between devices with their start and end apart: 1, of which 1 were waited for; matrix products, arithmetic and copies ran while one was open for 1% of the time, Pallas kernels for 0%

profile of v2, /device:TPU:0, one launch (start us, length us, event | category | flops | bytes accessed | tf_op | source)
XLA Modules:
  0.0 197.9 jit_solution(13128212586561462233)
XLA Ops:
  0.6 0.9 pad_maximum_fusion.3
  1.5 1.6 broadcast_in_dim.14
  3.1 0.0 copy-start.3
  3.1 0.0 copy-start.1
  3.1 0.0 copy-start.2
  3.1 8.5 %all-to-all-start = ((bf16[16,256,256]{2,1,0:T(8,128)(2,1)}), bf16[16,256,256]{2,1,0:T(8,128)(2,1)S(1)}, u32[]{:S(2)}, u32[]{:S(2)}) async-start(bf16[16,256,256]{2,1,0:T(8,128)(2,1)} %broadcast_in_dim.14), calls=%async_computation | async-start | bytes 4194304 | tf_op jit(solution)/shard_map/all_to_all | solution.py:87
  11.6 0.0 copy-done.3
  11.6 0.1 copy.33
  11.7 0.1 reduce-window.9
  11.8 0.1 reduce
  11.9 0.0 copy-done.1
  11.9 0.0 copy-done.2
  11.9 0.2 multiply_bitcast_fusion
  12.1 0.2 copy.41
  12.3 0.3 bitcast_reduce_fusion
  12.6 0.7 copy.37
  13.3 0.1 broadcast_multiply_fusion
  13.4 0.0 copy-start.4
  13.4 0.1 iota_add_fusion
  13.5 0.1 select_reduce_fusion
  13.6 0.1 slice_reduce_fusion
  13.7 0.6 subtract_maximum_fusion.kb0_ref
  14.2 40.4 %all-to-all-done = bf16[16,256,256]{2,1,0:T(8,128)(2,1)S(1)} async-done(((bf16[16,256,256]{2,1,0:T(8,128)(2,1)}), bf16[16,256,256]{2,1,0:T(8,128)(2,1)S(1)}, u32[]{:S(2)}, u32[]{:S(2)}) %all-to-all-start) | async-done | bytes 2097184 | tf_op jit(solution)/shard_map/all_to_all | solution.py:87
  54.6 0.1 slice_bitcast_fusion.1
  54.7 0.1 reverse_bitcast_fusion.1
  54.8 0.0 copy-done.4
  54.8 0.3 pad_maximum_fusion.1
  55.1 0.2 constant_dynamic-slice_fusion.1
  55.3 0.8 copy.35
  56.1 0.8 copy.36
  57.0 1.1 fusion.2.kt_ref
  58.1 1.6 pad_maximum_fusion.2
  59.6 4.1 %copy.38.kv_ref = bf16[2,17,128,256]{3,2,1,0:T(8,128)(2,1)} copy(bf16[2,17,128,256]{2,3,1,0:T(8,128)(2,1)} %pad_maximum_fusion.2) | data formatting | bytes 4456448 | tf_op jit(solution)/shard_map/stack | solution.py:92
  63.8 0.6 tile.18
  64.4 0.6 tile.16
  65.0 7.7 %shard_map.85 = (bf16[256,1024]{1,0:T(8,128)(2,1)}, f32[2,17,128,256]{3,2,1,0:T(8,128)}) custom-call(s32[2]{0:T(128)} %copy-done.4, s32[2]{0:T(128)} %subtract_maximum_fusion.kb0_ref, bf16[256,1024]{1,0:T(8,128)(2,1)} %q_ref.1, bf16[256,1024]{1,0:T(8,128)(2,1)} %do_ref.1, bf16[2,17,128,256]{3,2,1,0:T(8,128)(2,1)} %copy.38.kv_ref, ...), custom_call_target="tpu_custom_call" | custom-call | flops 6845104128 | bytes 8388608 | tf_op jit(solution)/shard_map/pallas_call | solution.py:136
  72.7 0.0 copy-start
  72.7 0.7 broadcast_in_dim.30
  73.5 1.5 copy-done
  75.0 0.2 bitcast_dynamic-update-slice_fusion
  75.2 0.5 fusion
  75.7 0.4 slice_bitcast_fusion
  76.2 0.2 reverse_bitcast_fusion
  76.4 0.4 pad_maximum_fusion
  76.8 0.4 copy.39
  77.3 117.5 %all_to_all.10 = f32[16,2,128,256]{3,2,1,0:T(8,128)} all-to-all(f32[16,2,128,256]{3,2,1,0:T(8,128)S(1)} %copy.39), channel_id=1, replica_groups=mesh['seq'=16,'grp'=2] {'seq'}, dimensions={0} | all-to-all | bytes 8388608 | tf_op jit(solution)/shard_map/all_to_all | solution.py:155
  194.7 2.5 %reduce_sum.19 = bf16[2,128,256]{2,1,0:T(8,128)(2,1)S(1)} reduce(f32[16,2,128,256]{3,2,1,0:T(8,128)} %all_to_all.10, f32[]{:T(128)} %constant.44.clone.1), dimensions={0}, to_apply=%region_3.4 | reduce | flops 983040 | bytes 4325380 | tf_op jit(solution)/shard_map/reduce_sum | solution.py:156
  197.2 0.7 fusion.3
  (3 shorter events, 0.0 us)
Async XLA Ops:
  3.1 8.5 %copy-start.3 = (s32[64]{0:T(128)S(1)}, s32[64]{0:T(128)}, u32[]{:S(2)}) copy-start(s32[64]{0:T(128)} %param.11) | copy-start | bytes 772
  3.1 8.8 %copy-start.1 = (bf16[256,1024]{1,0:T(8,128)(2,1)S(1)}, bf16[256,1024]{1,0:T(8,128)(2,1)}, u32[]{:S(2)}) copy-start(bf16[256,1024]{1,0:T(8,128)(2,1)} %param.9) | copy-start | bytes 1572868
  3.1 8.8 %copy-start.2 = (bf16[256,1024]{1,0:T(8,128)(2,1)S(1)}, bf16[256,1024]{1,0:T(8,128)(2,1)}, u32[]{:S(2)}) copy-start(bf16[256,1024]{1,0:T(8,128)(2,1)} %do_ref.1) | copy-start | bytes 1572868
  3.1 51.5 %all-to-all-start = ((bf16[16,256,256]{2,1,0:T(8,128)(2,1)}), bf16[16,256,256]{2,1,0:T(8,128)(2,1)S(1)}, u32[]{:S(2)}, u32[]{:S(2)}) async-start(bf16[16,256,256]{2,1,0:T(8,128)(2,1)} %broadcast_in_dim.14), calls=%async_computation | async-start | bytes 4194304 | tf_op jit(solution)/shard_map/all_to_all | solution.py:87
  13.4 41.4 %copy-start.4 = (s32[2]{0:T(128)}, s32[2]{0:T(128)S(1)}, u32[]{:S(2)}) copy-start(s32[2]{0:T(128)S(1)} %get-tuple-element.8.blk_ref) | copy-start | bytes 28
  72.7 2.3 %copy-start = (f32[2,17,128,256]{3,2,1,0:T(8,128)S(1)}, f32[2,17,128,256]{3,2,1,0:T(8,128)}, u32[]{:S(2)}) copy-start(f32[2,17,128,256]{3,2,1,0:T(8,128)} %get-tuple-element.6) | copy-start | bytes 13369348
